TPU v7x, 256 devices: a whole 4x4x8 slice. The times are simulated.
256 devices in a mesh: grp: 4 (over y_hi, core), tile: 64 (over y_lo, x, z).
Axes of the slice: x: 4, y: 4 (y_hi: 2, y_lo: 2; y = y_hi * 2 + y_lo), z: 8, core: 2. Of those that a mesh axis runs over, the one named last changes fastest.
Arguments:
- frames: float32 [4, 2048, 2048], P('grp', 'tile'), may hold values from -6 to 6
- otf: float32 [4, 2, 2048, 2048], P('grp', None, 'tile'), may hold values from -6 to 6, as said below
- start_image: float32 [2048, 2048], P('tile'), may hold values from -6 to 6
Outputs:
- consensus: float32 [2048, 2048], P('tile')
Inputs may be any that keep to these rules, and one draw needn't show every extreme that they name: Transfer functions of real point spread functions: otf[f, 0, t, s] equals otf[f, 0, -t, -s] and otf[f, 1, t, s] equals -otf[f, 1, -t, -s], indices taken modulo 2048.
All inputs are finite; a program needn't handle non-finite values.
Results may differ from a plain program's by a relative error of at most 0.0001.
Values sent between devices are 32-bit elements; how exact they have to be, the bound alone decides.
No kernel may reach another device: no remote copies, remote signals or barrier semaphores. Data moves between devices by JAX's collectives and lax.ppermute only.
A program may use at most 64 MiB of HBM per device.

v0:
```python
import math
import jax
import jax.numpy as jnp
from jax import lax
from jax.sharding import PartitionSpec as P

ITERS = 2
TV_ITERS = 4
penalty = 1.0
smooth_weight = 0.25
dual_step = 0.125
highest = lax.Precision.HIGHEST


def from_behind(value, axis, steps):
    count = lax.axis_size(axis)
    leading, last = (max(0, -steps), min(count, count - steps))
    return lax.ppermute(value, axis, [(source, source + steps) for source in range(leading, last)])


def angle_table(first_count, second_count, modulus):
    left_index = jnp.arange(first_count, dtype=jnp.int32)[:, None]
    right_index = jnp.arange(second_count, dtype=jnp.int32)[None, :]
    return (left_index * right_index % modulus).astype(jnp.float32) * (2.0 * math.pi / modulus)


def transform_last(real_part, imag_part, sign_value):
    extent = real_part.shape[-1]
    inner_size = 16
    outer_size = extent // inner_size
    leading = real_part.shape[:-1]
    first_angle = angle_table(inner_size, inner_size, inner_size)
    first_cos = jnp.cos(first_angle)
    first_sin = sign_value * jnp.sin(first_angle)
    split_real = real_part.reshape(leading + (inner_size, outer_size))
    mixed_real = jnp.einsum("...an,ak->...kn", split_real, first_cos, precision=highest)
    mixed_imag = jnp.einsum("...an,ak->...kn", split_real, first_sin, precision=highest)
    if imag_part is not None:
        split_imag = imag_part.reshape(leading + (inner_size, outer_size))
        mixed_real = mixed_real - jnp.einsum(
            "...an,ak->...kn", split_imag, first_sin, precision=highest
        )
        mixed_imag = mixed_imag + jnp.einsum(
            "...an,ak->...kn", split_imag, first_cos, precision=highest
        )
    twist_angle = angle_table(inner_size, outer_size, extent)
    twist_cos = jnp.cos(twist_angle)
    twist_sin = sign_value * jnp.sin(twist_angle)
    turned_real = mixed_real * twist_cos - mixed_imag * twist_sin
    turned_imag = mixed_real * twist_sin + mixed_imag * twist_cos
    second_angle = angle_table(outer_size, outer_size, outer_size)
    second_cos = jnp.cos(second_angle)
    second_sin = sign_value * jnp.sin(second_angle)
    out_real = jnp.einsum(
        "...kn,nj->...jk", turned_real, second_cos, precision=highest
    ) - jnp.einsum("...kn,nj->...jk", turned_imag, second_sin, precision=highest)
    out_imag = jnp.einsum(
        "...kn,nj->...jk", turned_real, second_sin, precision=highest
    ) + jnp.einsum("...kn,nj->...jk", turned_imag, second_cos, precision=highest)
    return (out_real.reshape(leading + (extent,)), out_imag.reshape(leading + (extent,)))


def regroup(moved, frame_count, tile_rows, extent):
    tiles = extent // tile_rows
    moved = moved.reshape(tile_rows, tiles, 2, frame_count, tile_rows)
    return jnp.transpose(moved, (2, 3, 0, 1, 4)).reshape(2, frame_count, tile_rows, extent)


def to_spectrum(images):
    frame_count, tile_rows, extent = images.shape
    col_real, col_imag = transform_last(images, None, -1.0)
    packed = jnp.transpose(jnp.stack([col_real, col_imag]), (3, 0, 1, 2)).reshape(
        extent, 2 * frame_count * tile_rows
    )
    moved = lax.all_to_all(packed, "tile", split_axis=0, concat_axis=1, tiled=True)
    moved = regroup(moved, frame_count, tile_rows, extent)
    return transform_last(moved[0], moved[1], -1.0)


def to_image(spec_real, spec_imag):
    frame_count, tile_rows, extent = spec_real.shape
    row_real, row_imag = transform_last(spec_real, spec_imag, 1.0)
    packed = jnp.transpose(jnp.stack([row_real, row_imag]), (3, 0, 1, 2)).reshape(
        extent, 2 * frame_count * tile_rows
    )
    moved = lax.all_to_all(packed, "tile", split_axis=0, concat_axis=1, tiled=True)
    moved = regroup(moved, frame_count, tile_rows, extent)
    image_parts = transform_last(moved[0], moved[1], 1.0)
    return image_parts[0] / float(extent * extent)


def denoise_sweeps(average):
    tile_rows, extent = average.shape
    on_last = lax.axis_index("tile") == lax.axis_size("tile") - 1
    row_index = jnp.arange(tile_rows, dtype=jnp.int32)[:, None]
    col_index = jnp.arange(extent, dtype=jnp.int32)[None, :]
    keep_rows = jnp.where((row_index == tile_rows - 1) & on_last, 0.0, 1.0).astype(jnp.float32)
    keep_cols = jnp.where(col_index == extent - 1, 0.0, 1.0).astype(jnp.float32)
    zero_col = jnp.zeros((tile_rows, 1), jnp.float32)

    def divergence(downward, sideways):
        above = from_behind(downward[-1:], "tile", 1)
        prev_rows = jnp.concatenate([above, downward[:-1]], 0)
        prev_cols = jnp.concatenate([zero_col, sideways[:, :-1]], 1)
        return downward - prev_rows + sideways - prev_cols

    downward = jnp.zeros_like(average)
    sideways = jnp.zeros_like(average)
    for sweep_index in range(TV_ITERS):
        target = divergence(downward, sideways) - average / smooth_weight
        below = from_behind(target[:1], "tile", -1)
        next_rows = jnp.concatenate([target[1:], below], 0)
        grad_down = (next_rows - target) * keep_rows
        grad_side = (jnp.concatenate([target[:, 1:], zero_col], 1) - target) * keep_cols
        grad_down, grad_side = (grad_down, grad_side)
        scaling = 1.0 + dual_step * jnp.sqrt(grad_down * grad_down + grad_side * grad_side)
        downward = (downward + dual_step * grad_down) / scaling
        sideways = (sideways + dual_step * grad_side) / scaling
    return average - smooth_weight * divergence(downward, sideways)


def denoise(average):
    return denoise_sweeps(average)


def body(frames, otf, start_image):
    frame_count = frames.shape[0]
    total_frames = float(frame_count * lax.axis_size("grp"))
    response_real = otf[:, 0]
    response_imag = otf[:, 1]
    gain = 1.0 / (response_real * response_real + response_imag * response_imag + penalty)
    data_real, data_imag = to_spectrum(frames)
    weighted_real = response_real * data_real + response_imag * data_imag
    weighted_imag = response_real * data_imag - response_imag * data_real
    consensus = start_image
    duals = jnp.zeros_like(frames)
    for iteration in range(ITERS):
        shifted_real, shifted_imag = to_spectrum(consensus[None] - duals)
        estimates = to_image(
            (weighted_real + penalty * shifted_real) * gain,
            (weighted_imag + penalty * shifted_imag) * gain,
        )
        partial_sum = jnp.sum(estimates + duals, axis=0)
        average = lax.psum(partial_sum, "grp") / total_frames
        consensus = denoise(average)
        duals = duals + estimates - consensus[None]
    return consensus


def solution(mesh):
    placed = (P("grp", "tile", None), P("grp", None, "tile", None), P("tile", None))
    return jax.shard_map(
        body, mesh=mesh, in_specs=placed, out_specs=P("tile", None), check_vma=False
    )
```

profile of v0, /device:TPU:8, one launch (start us, length us, event | category | flops | bytes accessed | tf_op | source)
XLA Modules:
  0.0 440.0 jit_solution(548711309243718294)
XLA Ops:
  6.6 1.0 copy.501
  13.4 1.1 copy.431
  14.5 1.4 reshape.646
  15.9 13.3 %all-to-all-start.1 = ((f32[64,1,2048]{2,1,0:T(1,128)}), f32[64,1,2048]{2,1,0:T(1,128)S(1)}, u32[]{:S(2)}, u32[]{:S(2)}) async-start(f32[64,1,2048]{2,1,0:T(1,128)} %reshape.646), calls=%async_computation.1 | async-start | bytes 1048576 | tf_op jit(solution)/shard_map/all_to_all | solution.py:75
  30.2 17.7 %all-to-all-done.1 = f32[64,1,2048]{2,1,0:T(1,128)S(1)} async-done(((f32[64,1,2048]{2,1,0:T(1,128)}), f32[64,1,2048]{2,1,0:T(1,128)S(1)}, u32[]{:S(2)}, u32[]{:S(2)}) %all-to-all-start.1) | async-done | bytes 524320 | tf_op jit(solution)/shard_map/all_to_all | solution.py:75
  48.5 1.9 reduce
  54.1 1.2 add_bitcast_fusion.6
  60.2 1.1 copy.411
  61.3 1.4 reshape.644
  62.8 5.0 %all-to-all-start = ((f32[64,1,2048]{2,1,0:T(1,128)}), f32[64,1,2048]{2,1,0:T(1,128)S(1)}, u32[]{:S(2)}, u32[]{:S(2)}) async-start(f32[64,1,2048]{2,1,0:T(1,128)} %reshape.644), calls=%async_computation | async-start | bytes 1048576 | tf_op jit(solution)/shard_map/all_to_all | solution.py:75
  73.8 12.0 %all-to-all-done = f32[64,1,2048]{2,1,0:T(1,128)S(1)} async-done(((f32[64,1,2048]{2,1,0:T(1,128)}), f32[64,1,2048]{2,1,0:T(1,128)S(1)}, u32[]{:S(2)}, u32[]{:S(2)}) %all-to-all-start) | async-done | bytes 524320 | tf_op jit(solution)/shard_map/all_to_all | solution.py:75
  85.8 1.9 reduce.1
  103.2 2.1 copy.453
  105.4 1.9 reshape.648
  107.3 22.4 %all_to_all.80 = f32[64,1,2048]{2,1,0:T(1,128)S(1)} all-to-all(f32[64,1,2048]{2,1,0:T(1,128)S(1)} %reshape.648), channel_id=1, replica_groups=mesh['grp'=4,'tile'=64] {'tile'}, dimensions={0} | all-to-all | bytes 1048576 | tf_op jit(solution)/shard_map/all_to_all | solution.py:86
  129.7 1.9 reduce.2
  137.5 1.0 copy.460
  138.6 2.8 collective-permute-start
  141.4 6.9 %collective-permute-done = f32[1,2048]{1,0:T(1,128)S(1)} collective-permute-done((f32[1,2048]{1,0:T(1,128)S(1)}, f32[1,2048]{1,0:T(1,128)S(1)}, u32[]{:S(2)}, u32[]{:S(2)}) %collective-permute-start) | collective-permute-done | bytes 8224 | tf_op jit(solution)/shard_map/ppermute | solution.py:18
  148.4 30.6 %all-reduce.20.cloned.1.call-done = f32[32,2048]{1,0:T(8,128)} async-done(((f32[32,2048]{1,0:T(8,128)}), f32[32,2048]{1,0:T(8,128)}) %all-reduce.20.cloned.1.call-update) | async-done | bytes 262160 | tf_op jit(solution)/shard_map/psum | solution.py:144
  179.0 1.0 fusion.80
  180.1 8.2 %collective-permute-start.1 = (f32[1,2048]{1,0:T(1,128)S(1)}, f32[1,2048]{1,0:T(1,128)S(1)}, u32[]{:S(2)}, u32[]{:S(2)}) collective-permute-start(f32[1,2048]{1,0:T(1,128)S(1)} %slice.257), channel_id=1, source_target_pairs={{1,0},{2,1},{3,2},{4,3},{5,4},{6,5},{7,6},{8,7},{9,8},{10,9},{11,1... | collective-permute-start | bytes 24584 | tf_op jit(solution)/shard_map/ppermute | solution.py:18
  188.5 1.2 collective-permute-done.1
  189.6 1.2 multiply_divide_fusion.3
  190.8 1.9 collective-permute-start.2
  192.8 8.1 %collective-permute-done.2 = f32[1,2048]{1,0:T(1,128)S(1)} collective-permute-done((f32[1,2048]{1,0:T(1,128)S(1)}, f32[1,2048]{1,0:T(1,128)S(1)}, u32[]{:S(2)}, u32[]{:S(2)}) %collective-permute-start.2) | collective-permute-done | bytes 8224 | tf_op jit(solution)/shard_map/ppermute | solution.py:18
  201.0 3.9 collective-permute-start.3
  205.1 1.5 collective-permute-done.3
  206.9 1.9 collective-permute-start.4
  208.8 7.8 %collective-permute-done.4 = f32[1,2048]{1,0:T(1,128)S(1)} collective-permute-done((f32[1,2048]{1,0:T(1,128)S(1)}, f32[1,2048]{1,0:T(1,128)S(1)}, u32[]{:S(2)}, u32[]{:S(2)}) %collective-permute-start.4) | collective-permute-done | bytes 8224 | tf_op jit(solution)/shard_map/ppermute | solution.py:18
  216.8 3.9 collective-permute-start.5
  220.9 1.5 collective-permute-done.5
  222.6 1.9 collective-permute-start.6
  224.6 7.8 %collective-permute-done.6 = f32[1,2048]{1,0:T(1,128)S(1)} collective-permute-done((f32[1,2048]{1,0:T(1,128)S(1)}, f32[1,2048]{1,0:T(1,128)S(1)}, u32[]{:S(2)}, u32[]{:S(2)}) %collective-permute-start.6) | collective-permute-done | bytes 8224 | tf_op jit(solution)/shard_map/ppermute | solution.py:18
  232.6 3.9 collective-permute-start.7
  236.6 1.5 collective-permute-done.7
  238.4 2.1 collective-permute-start.8
  240.5 7.6 %collective-permute-done.8 = f32[1,2048]{1,0:T(1,128)S(1)} collective-permute-done((f32[1,2048]{1,0:T(1,128)S(1)}, f32[1,2048]{1,0:T(1,128)S(1)}, u32[]{:S(2)}, u32[]{:S(2)}) %collective-permute-start.8) | collective-permute-done | bytes 8224 | tf_op jit(solution)/shard_map/ppermute | solution.py:18
  254.8 2.1 copy.470
  256.9 1.9 reshape.650
  258.8 18.9 %all_to_all.81 = f32[64,1,2048]{2,1,0:T(1,128)S(1)} all-to-all(f32[64,1,2048]{2,1,0:T(1,128)S(1)} %reshape.650), channel_id=1, replica_groups=mesh['grp'=4,'tile'=64] {'tile'}, dimensions={0} | all-to-all | bytes 1048576 | tf_op jit(solution)/shard_map/all_to_all | solution.py:75
  277.7 1.9 reduce.3
  294.7 1.1 copy.490
  296.5 19.3 %all_to_all.82 = f32[64,1,2048]{2,1,0:T(1,128)S(1)} all-to-all(f32[64,1,2048]{2,1,0:T(1,128)S(1)} %reshape.652), channel_id=1, replica_groups=mesh['grp'=4,'tile'=64] {'tile'}, dimensions={0} | all-to-all | bytes 1048576 | tf_op jit(solution)/shard_map/all_to_all | solution.py:86
  315.9 1.9 reduce.4
  324.8 38.2 %all-reduce.22.cloned.1.call-done = f32[32,2048]{1,0:T(8,128)} async-done(((f32[32,2048]{1,0:T(8,128)}), f32[32,2048]{1,0:T(8,128)}) %all-reduce.22.cloned.1.call-update) | async-done | bytes 262160 | tf_op jit(solution)/shard_map/psum | solution.py:144
  363.0 1.0 fusion.79
  364.1 8.2 %collective-permute-start.9 = (f32[1,2048]{1,0:T(1,128)S(1)}, f32[1,2048]{1,0:T(1,128)S(1)}, u32[]{:S(2)}, u32[]{:S(2)}) collective-permute-start(f32[1,2048]{1,0:T(1,128)S(1)} %slice.285), channel_id=1, source_target_pairs={{1,0},{2,1},{3,2},{4,3},{5,4},{6,5},{7,6},{8,7},{9,8},{10,9},{11,1... | collective-permute-start | bytes 24584 | tf_op jit(solution)/shard_map/ppermute | solution.py:18
  372.5 1.2 collective-permute-done.9
  373.7 1.2 multiply_divide_fusion.1
  374.9 1.9 collective-permute-start.10
  376.8 8.1 %collective-permute-done.10 = f32[1,2048]{1,0:T(1,128)S(1)} collective-permute-done((f32[1,2048]{1,0:T(1,128)S(1)}, f32[1,2048]{1,0:T(1,128)S(1)}, u32[]{:S(2)}, u32[]{:S(2)}) %collective-permute-start.10) | collective-permute-done | bytes 8224 | tf_op jit(solution)/shard_map/ppermute | solution.py:18
  385.1 3.9 collective-permute-start.11
  389.2 1.5 collective-permute-done.11
  390.9 1.9 collective-permute-start.12
  392.8 7.8 %collective-permute-done.12 = f32[1,2048]{1,0:T(1,128)S(1)} collective-permute-done((f32[1,2048]{1,0:T(1,128)S(1)}, f32[1,2048]{1,0:T(1,128)S(1)}, u32[]{:S(2)}, u32[]{:S(2)}) %collective-permute-start.12) | collective-permute-done | bytes 8224 | tf_op jit(solution)/shard_map/ppermute | solution.py:18
  400.8 3.9 collective-permute-start.13
  404.9 1.5 collective-permute-done.13
  406.6 1.9 collective-permute-start.14
  408.6 7.8 %collective-permute-done.14 = f32[1,2048]{1,0:T(1,128)S(1)} collective-permute-done((f32[1,2048]{1,0:T(1,128)S(1)}, f32[1,2048]{1,0:T(1,128)S(1)}, u32[]{:S(2)}, u32[]{:S(2)}) %collective-permute-start.14) | collective-permute-done | bytes 8224 | tf_op jit(solution)/shard_map/ppermute | solution.py:18
  416.6 3.9 collective-permute-start.15
  420.7 1.5 collective-permute-done.15
  422.4 1.9 collective-permute-start.16
  424.3 7.8 %collective-permute-done.16 = f32[1,2048]{1,0:T(1,128)S(1)} collective-permute-done((f32[1,2048]{1,0:T(1,128)S(1)}, f32[1,2048]{1,0:T(1,128)S(1)}, u32[]{:S(2)}, u32[]{:S(2)}) %collective-permute-start.16) | collective-permute-done | bytes 8224 | tf_op jit(solution)/shard_map/ppermute | solution.py:18
  (231 shorter events, 76.3 us)
Async XLA Ops:
  14.5 14.8 %copy-start.8 = (f32[1,32,2048]{2,1,0:T(8,128)S(1)}, f32[1,32,2048]{2,1,0:T(8,128)}, u32[]{:S(2)}) copy-start(f32[1,32,2048]{2,1,0:T(8,128)} %param.3) | copy-start | bytes 786436
  15.9 32.0 %all-to-all-start.1 = ((f32[64,1,2048]{2,1,0:T(1,128)}), f32[64,1,2048]{2,1,0:T(1,128)S(1)}, u32[]{:S(2)}, u32[]{:S(2)}) async-start(f32[64,1,2048]{2,1,0:T(1,128)} %reshape.646), calls=%async_computation.1 | async-start | bytes 1048576 | tf_op jit(solution)/shard_map/all_to_all | solution.py:75
  61.3 6.7 %copy-start.7 = (f32[1,2,32,2048]{3,2,1,0:T(8,128)S(1)}, f32[1,2,32,2048]{3,2,1,0:T(8,128)}, u32[]{:S(2)}) copy-start(f32[1,2,32,2048]{3,2,1,0:T(8,128)} %param.4) | copy-start | bytes 1572868
  61.3 8.3 %copy-start.2 = (f32[32,16,128]{2,1,0:T(8,128)S(1)}, f32[32,16,128]{2,1,0:T(8,128)}, u32[]{:S(2)}) copy-start(f32[32,16,128]{2,1,0:T(8,128)} %get-tuple-element.48) | copy-start | bytes 786436
  62.8 23.1 %all-to-all-start = ((f32[64,1,2048]{2,1,0:T(1,128)}), f32[64,1,2048]{2,1,0:T(1,128)S(1)}, u32[]{:S(2)}, u32[]{:S(2)}) async-start(f32[64,1,2048]{2,1,0:T(1,128)} %reshape.644), calls=%async_computation | async-start | bytes 1048576 | tf_op jit(solution)/shard_map/all_to_all | solution.py:75
  67.7 111.3 %all-reduce.20.cloned.1.call-start = ((), (), s32[]{:S(2)}) async-start(), calls=%async_computation.5 | async-start | bytes 524288 | tf_op jit(solution)/shard_map/psum | solution.py:144
  94.9 1.6 copy-start.4
  95.0 1.6 copy-start.5
  138.6 224.5 %all-reduce.22.cloned.1.call-start = ((), (), s32[]{:S(2)}) async-start(), calls=%async_computation.6 | async-start | bytes 524288 | tf_op jit(solution)/shard_map/psum | solution.py:144
  138.6 9.8 %collective-permute-start = (f32[1,2048]{1,0:T(1,128)S(1)}, f32[1,2048]{1,0:T(1,128)S(1)}, u32[]{:S(2)}, u32[]{:S(2)}) collective-permute-start(f32[1,2048]{1,0:T(1,128)S(1)} %broadcast.351), channel_id=1, source_target_pairs={{0,1},{1,2},{2,3},{3,4},{4,5},{5,6},{6,7},{7,8},{8,9},{9,10},{10,1... | collective-permute-start | bytes 24584 | tf_op jit(solution)/shard_map/ppermute | solution.py:18
  179.0 21.9 %copy-start.1 = (f32[32,2048]{1,0:T(8,128)S(1)}, f32[32,2048]{1,0:T(8,128)}, u32[]{:S(2)}) copy-start(f32[32,2048]{1,0:T(8,128)} %all-reduce.20.cloned.1.call-done) | copy-start | bytes 786436
  180.1 9.6 %collective-permute-start.1 = (f32[1,2048]{1,0:T(1,128)S(1)}, f32[1,2048]{1,0:T(1,128)S(1)}, u32[]{:S(2)}, u32[]{:S(2)}) collective-permute-start(f32[1,2048]{1,0:T(1,128)S(1)} %slice.257), channel_id=1, source_target_pairs={{1,0},{2,1},{3,2},{4,3},{5,4},{6,5},{7,6},{8,7},{9,8},{10,9},{11,1... | collective-permute-start | bytes 24584 | tf_op jit(solution)/shard_map/ppermute | solution.py:18
  190.8 10.0 %collective-permute-start.2 = (f32[1,2048]{1,0:T(1,128)S(1)}, f32[1,2048]{1,0:T(1,128)S(1)}, u32[]{:S(2)}, u32[]{:S(2)}) collective-permute-start(f32[1,2048]{1,0:T(1,128)S(1)} %slice.259), channel_id=1, source_target_pairs={{0,1},{1,2},{2,3},{3,4},{4,5},{5,6},{6,7},{7,8},{8,9},{9,10},{10,1... | collective-permute-start | bytes 24584 | tf_op jit(solution)/shard_map/ppermute | solution.py:18
  201.0 5.5 %collective-permute-start.3 = (f32[1,2048]{1,0:T(1,128)S(1)}, f32[1,2048]{1,0:T(1,128)S(1)}, u32[]{:S(2)}, u32[]{:S(2)}) collective-permute-start(f32[1,2048]{1,0:T(1,128)S(1)} %slice.263), channel_id=1, source_target_pairs={{1,0},{2,1},{3,2},{4,3},{5,4},{6,5},{7,6},{8,7},{9,8},{10,9},{11,1... | collective-permute-start | bytes 24584 | tf_op jit(solution)/shard_map/ppermute | solution.py:18
  206.9 9.8 %collective-permute-start.4 = (f32[1,2048]{1,0:T(1,128)S(1)}, f32[1,2048]{1,0:T(1,128)S(1)}, u32[]{:S(2)}, u32[]{:S(2)}) collective-permute-start(f32[1,2048]{1,0:T(1,128)S(1)} %slice.265), channel_id=1, source_target_pairs={{0,1},{1,2},{2,3},{3,4},{4,5},{5,6},{6,7},{7,8},{8,9},{9,10},{10,1... | collective-permute-start | bytes 24584 | tf_op jit(solution)/shard_map/ppermute | solution.py:18
  216.8 5.5 %collective-permute-start.5 = (f32[1,2048]{1,0:T(1,128)S(1)}, f32[1,2048]{1,0:T(1,128)S(1)}, u32[]{:S(2)}, u32[]{:S(2)}) collective-permute-start(f32[1,2048]{1,0:T(1,128)S(1)} %slice.269), channel_id=1, source_target_pairs={{1,0},{2,1},{3,2},{4,3},{5,4},{6,5},{7,6},{8,7},{9,8},{10,9},{11,1... | collective-permute-start | bytes 24584 | tf_op jit(solution)/shard_map/ppermute | solution.py:18
  222.6 9.8 %collective-permute-start.6 = (f32[1,2048]{1,0:T(1,128)S(1)}, f32[1,2048]{1,0:T(1,128)S(1)}, u32[]{:S(2)}, u32[]{:S(2)}) collective-permute-start(f32[1,2048]{1,0:T(1,128)S(1)} %slice.271), channel_id=1, source_target_pairs={{0,1},{1,2},{2,3},{3,4},{4,5},{5,6},{6,7},{7,8},{8,9},{9,10},{10,1... | collective-permute-start | bytes 24584 | tf_op jit(solution)/shard_map/ppermute | solution.py:18
  232.4 15.8 %copy-start.3 = (f32[32,2048]{1,0:T(8,128)S(1)}, f32[32,2048]{1,0:T(8,128)}, u32[]{:S(2)}) copy-start(f32[32,2048]{1,0:T(8,128)} %copy.460) | copy-start | bytes 786436
  232.6 5.5 %collective-permute-start.7 = (f32[1,2048]{1,0:T(1,128)S(1)}, f32[1,2048]{1,0:T(1,128)S(1)}, u32[]{:S(2)}, u32[]{:S(2)}) collective-permute-start(f32[1,2048]{1,0:T(1,128)S(1)} %slice.275), channel_id=1, source_target_pairs={{1,0},{2,1},{3,2},{4,3},{5,4},{6,5},{7,6},{8,7},{9,8},{10,9},{11,1... | collective-permute-start | bytes 24584 | tf_op jit(solution)/shard_map/ppermute | solution.py:18
  238.4 9.8 %collective-permute-start.8 = (f32[1,2048]{1,0:T(1,128)S(1)}, f32[1,2048]{1,0:T(1,128)S(1)}, u32[]{:S(2)}, u32[]{:S(2)}) collective-permute-start(f32[1,2048]{1,0:T(1,128)S(1)} %slice.277), channel_id=1, source_target_pairs={{0,1},{1,2},{2,3},{3,4},{4,5},{5,6},{6,7},{7,8},{8,9},{9,10},{10,1... | collective-permute-start | bytes 24584 | tf_op jit(solution)/shard_map/ppermute | solution.py:18
  321.9 2.1 copy-start.6
  363.0 21.9 %copy-start = (f32[32,2048]{1,0:T(8,128)S(1)}, f32[32,2048]{1,0:T(8,128)}, u32[]{:S(2)}) copy-start(f32[32,2048]{1,0:T(8,128)} %all-reduce.22.cloned.1.call-done) | copy-start | bytes 786436
  364.1 9.6 %collective-permute-start.9 = (f32[1,2048]{1,0:T(1,128)S(1)}, f32[1,2048]{1,0:T(1,128)S(1)}, u32[]{:S(2)}, u32[]{:S(2)}) collective-permute-start(f32[1,2048]{1,0:T(1,128)S(1)} %slice.285), channel_id=1, source_target_pairs={{1,0},{2,1},{3,2},{4,3},{5,4},{6,5},{7,6},{8,7},{9,8},{10,9},{11,1... | collective-permute-start | bytes 24584 | tf_op jit(solution)/shard_map/ppermute | solution.py:18
  374.9 10.0 %collective-permute-start.10 = (f32[1,2048]{1,0:T(1,128)S(1)}, f32[1,2048]{1,0:T(1,128)S(1)}, u32[]{:S(2)}, u32[]{:S(2)}) collective-permute-start(f32[1,2048]{1,0:T(1,128)S(1)} %slice.287), channel_id=1, source_target_pairs={{0,1},{1,2},{2,3},{3,4},{4,5},{5,6},{6,7},{7,8},{8,9},{9,10},{10,1... | collective-permute-start | bytes 24584 | tf_op jit(solution)/shard_map/ppermute | solution.py:18
  385.1 5.5 %collective-permute-start.11 = (f32[1,2048]{1,0:T(1,128)S(1)}, f32[1,2048]{1,0:T(1,128)S(1)}, u32[]{:S(2)}, u32[]{:S(2)}) collective-permute-start(f32[1,2048]{1,0:T(1,128)S(1)} %slice.291), channel_id=1, source_target_pairs={{1,0},{2,1},{3,2},{4,3},{5,4},{6,5},{7,6},{8,7},{9,8},{10,9},{11,1... | collective-permute-start | bytes 24584 | tf_op jit(solution)/shard_map/ppermute | solution.py:18
  390.9 9.8 %collective-permute-start.12 = (f32[1,2048]{1,0:T(1,128)S(1)}, f32[1,2048]{1,0:T(1,128)S(1)}, u32[]{:S(2)}, u32[]{:S(2)}) collective-permute-start(f32[1,2048]{1,0:T(1,128)S(1)} %slice.293), channel_id=1, source_target_pairs={{0,1},{1,2},{2,3},{3,4},{4,5},{5,6},{6,7},{7,8},{8,9},{9,10},{10,1... | collective-permute-start | bytes 24584 | tf_op jit(solution)/shard_map/ppermute | solution.py:18
  400.8 5.5 %collective-permute-start.13 = (f32[1,2048]{1,0:T(1,128)S(1)}, f32[1,2048]{1,0:T(1,128)S(1)}, u32[]{:S(2)}, u32[]{:S(2)}) collective-permute-start(f32[1,2048]{1,0:T(1,128)S(1)} %slice.297), channel_id=1, source_target_pairs={{1,0},{2,1},{3,2},{4,3},{5,4},{6,5},{7,6},{8,7},{9,8},{10,9},{11,1... | collective-permute-start | bytes 24584 | tf_op jit(solution)/shard_map/ppermute | solution.py:18
  406.6 9.8 %collective-permute-start.14 = (f32[1,2048]{1,0:T(1,128)S(1)}, f32[1,2048]{1,0:T(1,128)S(1)}, u32[]{:S(2)}, u32[]{:S(2)}) collective-permute-start(f32[1,2048]{1,0:T(1,128)S(1)} %slice.299), channel_id=1, source_target_pairs={{0,1},{1,2},{2,3},{3,4},{4,5},{5,6},{6,7},{7,8},{8,9},{9,10},{10,1... | collective-permute-start | bytes 24584 | tf_op jit(solution)/shard_map/ppermute | solution.py:18
  416.6 5.5 %collective-permute-start.15 = (f32[1,2048]{1,0:T(1,128)S(1)}, f32[1,2048]{1,0:T(1,128)S(1)}, u32[]{:S(2)}, u32[]{:S(2)}) collective-permute-start(f32[1,2048]{1,0:T(1,128)S(1)} %slice.303), channel_id=1, source_target_pairs={{1,0},{2,1},{3,2},{4,3},{5,4},{6,5},{7,6},{8,7},{9,8},{10,9},{11,1... | collective-permute-start | bytes 24584 | tf_op jit(solution)/shard_map/ppermute | solution.py:18
  422.4 9.8 %collective-permute-start.16 = (f32[1,2048]{1,0:T(1,128)S(1)}, f32[1,2048]{1,0:T(1,128)S(1)}, u32[]{:S(2)}, u32[]{:S(2)}) collective-permute-start(f32[1,2048]{1,0:T(1,128)S(1)} %slice.305), channel_id=1, source_target_pairs={{0,1},{1,2},{2,3},{3,4},{4,5},{5,6},{6,7},{7,8},{8,9},{9,10},{10,1... | collective-permute-start | bytes 24584 | tf_op jit(solution)/shard_map/ppermute | solution.py:18
Sparse Core Ops, SparseCore 0:
  138.7 40.2 all-reduce.19
  324.9 38.0 all-reduce.21
where the time goes:
time: 447 us; the launch traced here: 440 us
  waiting for transfers between devices  180 us (40%)
  starting transfers between devices  76.9 us (17%)
  blocking collectives  60.6 us (14%)
  local copies, waits for them, and re-layouts  50.5 us (11%)
  matrix products  37.6 us (8%)
  other arithmetic  19.4 us (4%)
  between operations  15.3 us (3%)
    ppermute x17, waiting for transfers between devices, from_behind(): lax.ppermute(value, axis, [(source, source + steps) for source in range(l...  81 us
    psum x2, waiting for transfers between devices, body(): average = lax.psum(partial_sum, 'grp') / total_frames  68.9 us
    ppermute x17, starting transfers between devices, from_behind(): lax.ppermute(value, axis, [(source, source + steps) for source in range(l...  58.4 us
    all_to_all x2, blocking collectives, to_image(): lax.all_to_all(packed, 'tile', split_axis=0, concat_axis=1, tiled=True)  41.8 us
    all_to_all x2, waiting for transfers between devices, to_spectrum(): lax.all_to_all(packed, 'tile', split_axis=0, concat_axis=1, tiled=True)  29.7 us
    all_to_all x1, blocking collectives, to_spectrum(): lax.all_to_all(packed, 'tile', split_axis=0, concat_axis=1, tiled=True)  18.9 us
    all_to_all x2, starting transfers between devices, to_spectrum(): lax.all_to_all(packed, 'tile', split_axis=0, concat_axis=1, tiled=True)  18.3 us
    unnamed x34, local copies, waits for them, and re-layouts  12 us
  transfers between devices with their start and end apart: 21, of which 21 were waited for; matrix products, arithmetic and copies ran while one was open for 2% of the time, Pallas kernels for 0%

commit v1 on v0

--- a/solution.py
+++ b/solution.py
@@ -141,7 +141,7 @@
             (weighted_imag + penalty * shifted_imag) * gain,
         )
         partial_sum = jnp.sum(estimates + duals, axis=0)
-        average = lax.psum(partial_sum, "grp") / total_frames
+        average = jnp.sum(lax.all_gather(partial_sum, "grp"), axis=0) / total_frames
         consensus = denoise(average)
         duals = duals + estimates - consensus[None]
     return consensus

time: 447 us -> 400 us (0.89)
  waiting for transfers between devices: 180 us -> 134 us
    psum x2 -> x0, waiting for transfers between devices: 68.9 us -> none  [body(): average = lax.psum(partial_sum, 'grp') / total_frames]
    all_gather x0 -> x2, waiting for transfers between devices: none -> 30.8 us  [body(): average = jnp.sum(lax.all_gather(partial_sum, 'grp'), axis=0) / total_frames]
    ppermute x17, waiting for transfers between devices: 81 us -> 73.8 us  [from_behind(): lax.ppermute(value, axis, [(source, source + steps) for source in range(l...]
    unnamed x34 -> x28, local copies, waits for them, and re-layouts: 12 us -> 12 us
  transfers between devices with their start and end apart: 21 -> 21, of which waited for: 21 -> 20; matrix products, arithmetic and copies ran while one was open for 2% -> 2% of each run, Pallas kernels for 0% -> 0%
where the time goes in v1:
time: 400 us; the launch traced here: 394 us
  waiting for transfers between devices  134 us (34%)
  starting transfers between devices  77 us (19%)
  blocking collectives  60.6 us (15%)
  local copies, waits for them, and re-layouts  50.8 us (13%)
  matrix products  37.6 us (9%)
  other arithmetic  17.8 us (4%)
  between operations  15.4 us (4%)
    ppermute x17, waiting for transfers between devices, from_behind(): lax.ppermute(value, axis, [(source, source + steps) for source in range(l...  73.8 us
    ppermute x17, starting transfers between devices, from_behind(): lax.ppermute(value, axis, [(source, source + steps) for source in range(l...  58.4 us
    all_to_all x2, blocking collectives, to_image(): lax.all_to_all(packed, 'tile', split_axis=0, concat_axis=1, tiled=True)  41.7 us
    all_gather x2, waiting for transfers between devices, body(): average = jnp.sum(lax.all_gather(partial_sum, 'grp'), axis=0) / total_frames  30.8 us
    all_to_all x2, waiting for transfers between devices, to_spectrum(): lax.all_to_all(packed, 'tile', split_axis=0, concat_axis=1, tiled=True)  29.7 us
    all_to_all x1, blocking collectives, to_spectrum(): lax.all_to_all(packed, 'tile', split_axis=0, concat_axis=1, tiled=True)  18.9 us
    all_to_all x2, starting transfers between devices, to_spectrum(): lax.all_to_all(packed, 'tile', split_axis=0, concat_axis=1, tiled=True)  18.3 us
    unnamed x28, local copies, waits for them, and re-layouts  12 us
  transfers between devices with their start and end apart: 21, of which 20 were waited for; matrix products, arithmetic and copies ran while one was open for 2% of the time, Pallas kernels for 0%

profile of v1, /device:TPU:8, one launch (start us, length us, event | category | flops | bytes accessed | tf_op | source)
XLA Modules:
  0.0 393.5 jit_solution(18265783277875700476)
XLA Ops:
  6.6 1.0 copy.414
  13.4 1.1 copy.343
  14.5 1.5 reshape.661
  16.0 13.3 %all-to-all-start.1 = ((f32[64,1,2048]{2,1,0:T(1,128)}), f32[64,1,2048]{2,1,0:T(1,128)S(1)}, u32[]{:S(2)}, u32[]{:S(2)}) async-start(f32[64,1,2048]{2,1,0:T(1,128)} %reshape.661), calls=%async_computation.1 | async-start | bytes 1048576 | tf_op jit(solution)/shard_map/all_to_all | solution.py:75
  30.2 17.7 %all-to-all-done.1 = f32[64,1,2048]{2,1,0:T(1,128)S(1)} async-done(((f32[64,1,2048]{2,1,0:T(1,128)}), f32[64,1,2048]{2,1,0:T(1,128)S(1)}, u32[]{:S(2)}, u32[]{:S(2)}) %all-to-all-start.1) | async-done | bytes 524320 | tf_op jit(solution)/shard_map/all_to_all | solution.py:75
  48.5 1.9 reduce
  54.1 1.2 add_bitcast_fusion.6
  60.1 1.1 copy.323
  61.3 1.4 reshape.659
  62.7 5.0 %all-to-all-start = ((f32[64,1,2048]{2,1,0:T(1,128)}), f32[64,1,2048]{2,1,0:T(1,128)S(1)}, u32[]{:S(2)}, u32[]{:S(2)}) async-start(f32[64,1,2048]{2,1,0:T(1,128)} %reshape.659), calls=%async_computation | async-start | bytes 1048576 | tf_op jit(solution)/shard_map/all_to_all | solution.py:75
  68.8 0.8 copy.413
  73.8 12.0 %all-to-all-done = f32[64,1,2048]{2,1,0:T(1,128)S(1)} async-done(((f32[64,1,2048]{2,1,0:T(1,128)}), f32[64,1,2048]{2,1,0:T(1,128)S(1)}, u32[]{:S(2)}, u32[]{:S(2)}) %all-to-all-start) | async-done | bytes 524320 | tf_op jit(solution)/shard_map/all_to_all | solution.py:75
  85.8 1.9 reduce.1
  103.2 2.1 copy.365
  105.3 1.9 reshape.663
  107.2 22.4 %all_to_all.80 = f32[64,1,2048]{2,1,0:T(1,128)S(1)} all-to-all(f32[64,1,2048]{2,1,0:T(1,128)S(1)} %reshape.663), channel_id=1, replica_groups=mesh['grp'=4,'tile'=64] {'tile'}, dimensions={0} | all-to-all | bytes 1048576 | tf_op jit(solution)/shard_map/all_to_all | solution.py:86
  129.6 1.9 reduce.2
  137.4 1.0 copy.372
  138.5 2.8 collective-permute-start
  141.3 15.1 %all-gather.4.cloned.1.call-done = f32[4,32,2048]{2,1,0:T(8,128)} async-done(((f32[1,32,2048]{2,1,0:T(8,128)}), f32[4,32,2048]{2,1,0:T(8,128)}) %all-gather.4.cloned.1.call-update) | async-done | bytes 1048592 | tf_op jit(solution)/shard_map/all_gather | solution.py:144
  156.4 1.3 reduce_sum.16
  157.8 8.2 %collective-permute-start.1 = (f32[1,2048]{1,0:T(1,128)S(1)}, f32[1,2048]{1,0:T(1,128)S(1)}, u32[]{:S(2)}, u32[]{:S(2)}) collective-permute-start(f32[1,2048]{1,0:T(1,128)S(1)} %slice.257), channel_id=1, source_target_pairs={{1,0},{2,1},{3,2},{4,3},{5,4},{6,5},{7,6},{8,7},{9,8},{10,9},{11,1... | collective-permute-start | bytes 24584 | tf_op jit(solution)/shard_map/ppermute | solution.py:18
  166.2 1.2 collective-permute-done.1
  167.6 1.9 collective-permute-start.2
  169.5 8.1 %collective-permute-done.2 = f32[1,2048]{1,0:T(1,128)S(1)} collective-permute-done((f32[1,2048]{1,0:T(1,128)S(1)}, f32[1,2048]{1,0:T(1,128)S(1)}, u32[]{:S(2)}, u32[]{:S(2)}) %collective-permute-start.2) | collective-permute-done | bytes 8224 | tf_op jit(solution)/shard_map/ppermute | solution.py:18
  177.8 3.9 collective-permute-start.3
  181.9 1.5 collective-permute-done.3
  183.6 1.9 collective-permute-start.4
  185.6 7.8 %collective-permute-done.4 = f32[1,2048]{1,0:T(1,128)S(1)} collective-permute-done((f32[1,2048]{1,0:T(1,128)S(1)}, f32[1,2048]{1,0:T(1,128)S(1)}, u32[]{:S(2)}, u32[]{:S(2)}) %collective-permute-start.4) | collective-permute-done | bytes 8224 | tf_op jit(solution)/shard_map/ppermute | solution.py:18
  193.6 3.9 collective-permute-start.5
  197.7 1.5 collective-permute-done.5
  199.4 1.9 collective-permute-start.6
  201.3 7.8 %collective-permute-done.6 = f32[1,2048]{1,0:T(1,128)S(1)} collective-permute-done((f32[1,2048]{1,0:T(1,128)S(1)}, f32[1,2048]{1,0:T(1,128)S(1)}, u32[]{:S(2)}, u32[]{:S(2)}) %collective-permute-start.6) | collective-permute-done | bytes 8224 | tf_op jit(solution)/shard_map/ppermute | solution.py:18
  209.3 3.9 collective-permute-start.7
  213.4 1.5 collective-permute-done.7
  215.1 2.1 collective-permute-start.8
  217.6 7.3 %collective-permute-done.8 = f32[1,2048]{1,0:T(1,128)S(1)} collective-permute-done((f32[1,2048]{1,0:T(1,128)S(1)}, f32[1,2048]{1,0:T(1,128)S(1)}, u32[]{:S(2)}, u32[]{:S(2)}) %collective-permute-start.8) | collective-permute-done | bytes 8224 | tf_op jit(solution)/shard_map/ppermute | solution.py:18
  224.9 0.9 subtract_bitcast_fusion.4
  231.6 2.1 copy.383
  233.7 1.9 reshape.665
  235.6 18.9 %all_to_all.81 = f32[64,1,2048]{2,1,0:T(1,128)S(1)} all-to-all(f32[64,1,2048]{2,1,0:T(1,128)S(1)} %reshape.665), channel_id=1, replica_groups=mesh['grp'=4,'tile'=64] {'tile'}, dimensions={0} | all-to-all | bytes 1048576 | tf_op jit(solution)/shard_map/all_to_all | solution.py:75
  254.4 1.9 reduce.3
  271.4 1.1 copy.403
  273.2 19.3 %all_to_all.82 = f32[64,1,2048]{2,1,0:T(1,128)S(1)} all-to-all(f32[64,1,2048]{2,1,0:T(1,128)S(1)} %reshape.667), channel_id=1, replica_groups=mesh['grp'=4,'tile'=64] {'tile'}, dimensions={0} | all-to-all | bytes 1048576 | tf_op jit(solution)/shard_map/all_to_all | solution.py:86
  292.5 1.9 reduce.4
  301.4 15.8 %all-gather.6.cloned.1.call-done = f32[128,2048]{1,0:T(8,128)} async-done(((f32[32,2048]{1,0:T(8,128)}), f32[128,2048]{1,0:T(8,128)}) %all-gather.6.cloned.1.call-update) | async-done | bytes 1048592 | tf_op jit(solution)/shard_map/all_gather | solution.py:144
  317.2 1.3 reduce_sum.20
  318.5 8.2 %collective-permute-start.9 = (f32[1,2048]{1,0:T(1,128)S(1)}, f32[1,2048]{1,0:T(1,128)S(1)}, u32[]{:S(2)}, u32[]{:S(2)}) collective-permute-start(f32[1,2048]{1,0:T(1,128)S(1)} %slice.285), channel_id=1, source_target_pairs={{1,0},{2,1},{3,2},{4,3},{5,4},{6,5},{7,6},{8,7},{9,8},{10,9},{11,1... | collective-permute-start | bytes 24584 | tf_op jit(solution)/shard_map/ppermute | solution.py:18
  326.9 1.2 collective-permute-done.9
  328.4 1.9 collective-permute-start.10
  330.3 8.1 %collective-permute-done.10 = f32[1,2048]{1,0:T(1,128)S(1)} collective-permute-done((f32[1,2048]{1,0:T(1,128)S(1)}, f32[1,2048]{1,0:T(1,128)S(1)}, u32[]{:S(2)}, u32[]{:S(2)}) %collective-permute-start.10) | collective-permute-done | bytes 8224 | tf_op jit(solution)/shard_map/ppermute | solution.py:18
  338.6 3.9 collective-permute-start.11
  342.7 1.5 collective-permute-done.11
  344.4 1.9 collective-permute-start.12
  346.3 7.8 %collective-permute-done.12 = f32[1,2048]{1,0:T(1,128)S(1)} collective-permute-done((f32[1,2048]{1,0:T(1,128)S(1)}, f32[1,2048]{1,0:T(1,128)S(1)}, u32[]{:S(2)}, u32[]{:S(2)}) %collective-permute-start.12) | collective-permute-done | bytes 8224 | tf_op jit(solution)/shard_map/ppermute | solution.py:18
  354.3 3.9 collective-permute-start.13
  358.4 1.5 collective-permute-done.13
  360.2 1.9 collective-permute-start.14
  362.1 7.8 %collective-permute-done.14 = f32[1,2048]{1,0:T(1,128)S(1)} collective-permute-done((f32[1,2048]{1,0:T(1,128)S(1)}, f32[1,2048]{1,0:T(1,128)S(1)}, u32[]{:S(2)}, u32[]{:S(2)}) %collective-permute-start.14) | collective-permute-done | bytes 8224 | tf_op jit(solution)/shard_map/ppermute | solution.py:18
  370.1 3.9 collective-permute-start.15
  374.2 1.5 collective-permute-done.15
  375.9 1.9 collective-permute-start.16
  377.8 7.8 %collective-permute-done.16 = f32[1,2048]{1,0:T(1,128)S(1)} collective-permute-done((f32[1,2048]{1,0:T(1,128)S(1)}, f32[1,2048]{1,0:T(1,128)S(1)}, u32[]{:S(2)}, u32[]{:S(2)}) %collective-permute-start.16) | collective-permute-done | bytes 8224 | tf_op jit(solution)/shard_map/ppermute | solution.py:18
  385.7 0.8 fusion.72
  (228 shorter events, 74.7 us)
Async XLA Ops:
  14.5 14.8 %copy-start.5 = (f32[1,32,2048]{2,1,0:T(8,128)S(1)}, f32[1,32,2048]{2,1,0:T(8,128)}, u32[]{:S(2)}) copy-start(f32[1,32,2048]{2,1,0:T(8,128)} %param.3) | copy-start | bytes 786436
  16.0 32.0 %all-to-all-start.1 = ((f32[64,1,2048]{2,1,0:T(1,128)}), f32[64,1,2048]{2,1,0:T(1,128)S(1)}, u32[]{:S(2)}, u32[]{:S(2)}) async-start(f32[64,1,2048]{2,1,0:T(1,128)} %reshape.661), calls=%async_computation.1 | async-start | bytes 1048576 | tf_op jit(solution)/shard_map/all_to_all | solution.py:75
  61.3 6.7 %copy-start.4 = (f32[1,2,32,2048]{3,2,1,0:T(8,128)S(1)}, f32[1,2,32,2048]{3,2,1,0:T(8,128)}, u32[]{:S(2)}) copy-start(f32[1,2,32,2048]{3,2,1,0:T(8,128)} %param.4) | copy-start | bytes 1572868
  61.3 8.3 %copy-start = (f32[32,16,128]{2,1,0:T(8,128)S(1)}, f32[32,16,128]{2,1,0:T(8,128)}, u32[]{:S(2)}) copy-start(f32[32,16,128]{2,1,0:T(8,128)} %get-tuple-element.48) | copy-start | bytes 786436
  62.7 23.1 %all-to-all-start = ((f32[64,1,2048]{2,1,0:T(1,128)}), f32[64,1,2048]{2,1,0:T(1,128)S(1)}, u32[]{:S(2)}, u32[]{:S(2)}) async-start(f32[64,1,2048]{2,1,0:T(1,128)} %reshape.659), calls=%async_computation | async-start | bytes 1048576 | tf_op jit(solution)/shard_map/all_to_all | solution.py:75
  67.7 88.7 %all-gather.4.cloned.1.call-start = ((), (), s32[]{:S(2)}) async-start(), calls=%async_computation.5 | async-start | bytes 1310720 | tf_op jit(solution)/shard_map/all_gather | solution.py:144
  94.9 1.6 copy-start.1
  94.9 1.6 copy-start.2
  138.4 178.7 %all-gather.6.cloned.1.call-start = ((), (), s32[]{:S(2)}) async-start(), calls=%async_computation.6 | async-start | bytes 1310720 | tf_op jit(solution)/shard_map/all_gather | solution.py:144
  138.5 19.2 %collective-permute-start = (f32[1,2048]{1,0:T(1,128)S(1)}, f32[1,2048]{1,0:T(1,128)S(1)}, u32[]{:S(2)}, u32[]{:S(2)}) collective-permute-start(f32[1,2048]{1,0:T(1,128)S(1)} %broadcast.363), channel_id=1, source_target_pairs={{0,1},{1,2},{2,3},{3,4},{4,5},{5,6},{6,7},{7,8},{8,9},{9,10},{10,1... | collective-permute-start | bytes 24584 | tf_op jit(solution)/shard_map/ppermute | solution.py:18
  157.8 9.6 %collective-permute-start.1 = (f32[1,2048]{1,0:T(1,128)S(1)}, f32[1,2048]{1,0:T(1,128)S(1)}, u32[]{:S(2)}, u32[]{:S(2)}) collective-permute-start(f32[1,2048]{1,0:T(1,128)S(1)} %slice.257), channel_id=1, source_target_pairs={{1,0},{2,1},{3,2},{4,3},{5,4},{6,5},{7,6},{8,7},{9,8},{10,9},{11,1... | collective-permute-start | bytes 24584 | tf_op jit(solution)/shard_map/ppermute | solution.py:18
  167.6 10.0 %collective-permute-start.2 = (f32[1,2048]{1,0:T(1,128)S(1)}, f32[1,2048]{1,0:T(1,128)S(1)}, u32[]{:S(2)}, u32[]{:S(2)}) collective-permute-start(f32[1,2048]{1,0:T(1,128)S(1)} %slice.259), channel_id=1, source_target_pairs={{0,1},{1,2},{2,3},{3,4},{4,5},{5,6},{6,7},{7,8},{8,9},{9,10},{10,1... | collective-permute-start | bytes 24584 | tf_op jit(solution)/shard_map/ppermute | solution.py:18
  177.8 5.5 %collective-permute-start.3 = (f32[1,2048]{1,0:T(1,128)S(1)}, f32[1,2048]{1,0:T(1,128)S(1)}, u32[]{:S(2)}, u32[]{:S(2)}) collective-permute-start(f32[1,2048]{1,0:T(1,128)S(1)} %slice.263), channel_id=1, source_target_pairs={{1,0},{2,1},{3,2},{4,3},{5,4},{6,5},{7,6},{8,7},{9,8},{10,9},{11,1... | collective-permute-start | bytes 24584 | tf_op jit(solution)/shard_map/ppermute | solution.py:18
  183.6 9.8 %collective-permute-start.4 = (f32[1,2048]{1,0:T(1,128)S(1)}, f32[1,2048]{1,0:T(1,128)S(1)}, u32[]{:S(2)}, u32[]{:S(2)}) collective-permute-start(f32[1,2048]{1,0:T(1,128)S(1)} %slice.265), channel_id=1, source_target_pairs={{0,1},{1,2},{2,3},{3,4},{4,5},{5,6},{6,7},{7,8},{8,9},{9,10},{10,1... | collective-permute-start | bytes 24584 | tf_op jit(solution)/shard_map/ppermute | solution.py:18
  193.6 5.5 %collective-permute-start.5 = (f32[1,2048]{1,0:T(1,128)S(1)}, f32[1,2048]{1,0:T(1,128)S(1)}, u32[]{:S(2)}, u32[]{:S(2)}) collective-permute-start(f32[1,2048]{1,0:T(1,128)S(1)} %slice.269), channel_id=1, source_target_pairs={{1,0},{2,1},{3,2},{4,3},{5,4},{6,5},{7,6},{8,7},{9,8},{10,9},{11,1... | collective-permute-start | bytes 24584 | tf_op jit(solution)/shard_map/ppermute | solution.py:18
  199.4 9.8 %collective-permute-start.6 = (f32[1,2048]{1,0:T(1,128)S(1)}, f32[1,2048]{1,0:T(1,128)S(1)}, u32[]{:S(2)}, u32[]{:S(2)}) collective-permute-start(f32[1,2048]{1,0:T(1,128)S(1)} %slice.271), channel_id=1, source_target_pairs={{0,1},{1,2},{2,3},{3,4},{4,5},{5,6},{6,7},{7,8},{8,9},{9,10},{10,1... | collective-permute-start | bytes 24584 | tf_op jit(solution)/shard_map/ppermute | solution.py:18
  209.3 5.5 %collective-permute-start.7 = (f32[1,2048]{1,0:T(1,128)S(1)}, f32[1,2048]{1,0:T(1,128)S(1)}, u32[]{:S(2)}, u32[]{:S(2)}) collective-permute-start(f32[1,2048]{1,0:T(1,128)S(1)} %slice.275), channel_id=1, source_target_pairs={{1,0},{2,1},{3,2},{4,3},{5,4},{6,5},{7,6},{8,7},{9,8},{10,9},{11,1... | collective-permute-start | bytes 24584 | tf_op jit(solution)/shard_map/ppermute | solution.py:18
  215.1 9.8 %collective-permute-start.8 = (f32[1,2048]{1,0:T(1,128)S(1)}, f32[1,2048]{1,0:T(1,128)S(1)}, u32[]{:S(2)}, u32[]{:S(2)}) collective-permute-start(f32[1,2048]{1,0:T(1,128)S(1)} %slice.277), channel_id=1, source_target_pairs={{0,1},{1,2},{2,3},{3,4},{4,5},{5,6},{6,7},{7,8},{8,9},{9,10},{10,1... | collective-permute-start | bytes 24584 | tf_op jit(solution)/shard_map/ppermute | solution.py:18
  298.6 2.1 copy-start.3
  318.5 9.6 %collective-permute-start.9 = (f32[1,2048]{1,0:T(1,128)S(1)}, f32[1,2048]{1,0:T(1,128)S(1)}, u32[]{:S(2)}, u32[]{:S(2)}) collective-permute-start(f32[1,2048]{1,0:T(1,128)S(1)} %slice.285), channel_id=1, source_target_pairs={{1,0},{2,1},{3,2},{4,3},{5,4},{6,5},{7,6},{8,7},{9,8},{10,9},{11,1... | collective-permute-start | bytes 24584 | tf_op jit(solution)/shard_map/ppermute | solution.py:18
  328.4 10.0 %collective-permute-start.10 = (f32[1,2048]{1,0:T(1,128)S(1)}, f32[1,2048]{1,0:T(1,128)S(1)}, u32[]{:S(2)}, u32[]{:S(2)}) collective-permute-start(f32[1,2048]{1,0:T(1,128)S(1)} %slice.287), channel_id=1, source_target_pairs={{0,1},{1,2},{2,3},{3,4},{4,5},{5,6},{6,7},{7,8},{8,9},{9,10},{10,1... | collective-permute-start | bytes 24584 | tf_op jit(solution)/shard_map/ppermute | solution.py:18
  338.6 5.5 %collective-permute-start.11 = (f32[1,2048]{1,0:T(1,128)S(1)}, f32[1,2048]{1,0:T(1,128)S(1)}, u32[]{:S(2)}, u32[]{:S(2)}) collective-permute-start(f32[1,2048]{1,0:T(1,128)S(1)} %slice.291), channel_id=1, source_target_pairs={{1,0},{2,1},{3,2},{4,3},{5,4},{6,5},{7,6},{8,7},{9,8},{10,9},{11,1... | collective-permute-start | bytes 24584 | tf_op jit(solution)/shard_map/ppermute | solution.py:18
  344.4 9.8 %collective-permute-start.12 = (f32[1,2048]{1,0:T(1,128)S(1)}, f32[1,2048]{1,0:T(1,128)S(1)}, u32[]{:S(2)}, u32[]{:S(2)}) collective-permute-start(f32[1,2048]{1,0:T(1,128)S(1)} %slice.293), channel_id=1, source_target_pairs={{0,1},{1,2},{2,3},{3,4},{4,5},{5,6},{6,7},{7,8},{8,9},{9,10},{10,1... | collective-permute-start | bytes 24584 | tf_op jit(solution)/shard_map/ppermute | solution.py:18
  354.3 5.5 %collective-permute-start.13 = (f32[1,2048]{1,0:T(1,128)S(1)}, f32[1,2048]{1,0:T(1,128)S(1)}, u32[]{:S(2)}, u32[]{:S(2)}) collective-permute-start(f32[1,2048]{1,0:T(1,128)S(1)} %slice.297), channel_id=1, source_target_pairs={{1,0},{2,1},{3,2},{4,3},{5,4},{6,5},{7,6},{8,7},{9,8},{10,9},{11,1... | collective-permute-start | bytes 24584 | tf_op jit(solution)/shard_map/ppermute | solution.py:18
  360.2 9.8 %collective-permute-start.14 = (f32[1,2048]{1,0:T(1,128)S(1)}, f32[1,2048]{1,0:T(1,128)S(1)}, u32[]{:S(2)}, u32[]{:S(2)}) collective-permute-start(f32[1,2048]{1,0:T(1,128)S(1)} %slice.299), channel_id=1, source_target_pairs={{0,1},{1,2},{2,3},{3,4},{4,5},{5,6},{6,7},{7,8},{8,9},{9,10},{10,1... | collective-permute-start | bytes 24584 | tf_op jit(solution)/shard_map/ppermute | solution.py:18
  370.1 5.5 %collective-permute-start.15 = (f32[1,2048]{1,0:T(1,128)S(1)}, f32[1,2048]{1,0:T(1,128)S(1)}, u32[]{:S(2)}, u32[]{:S(2)}) collective-permute-start(f32[1,2048]{1,0:T(1,128)S(1)} %slice.303), channel_id=1, source_target_pairs={{1,0},{2,1},{3,2},{4,3},{5,4},{6,5},{7,6},{8,7},{9,8},{10,9},{11,1... | collective-permute-start | bytes 24584 | tf_op jit(solution)/shard_map/ppermute | solution.py:18
  375.9 9.8 %collective-permute-start.16 = (f32[1,2048]{1,0:T(1,128)S(1)}, f32[1,2048]{1,0:T(1,128)S(1)}, u32[]{:S(2)}, u32[]{:S(2)}) collective-permute-start(f32[1,2048]{1,0:T(1,128)S(1)} %slice.305), channel_id=1, source_target_pairs={{0,1},{1,2},{2,3},{3,4},{4,5},{5,6},{6,7},{7,8},{8,9},{9,10},{10,1... | collective-permute-start | bytes 24584 | tf_op jit(solution)/shard_map/ppermute | solution.py:18
Sparse Core Ops, SparseCore 0:
  138.6 17.8 all-gather.3
  301.5 15.5 all-gather.5
